TPU v7x, 32 devices: a whole 2x2x4 slice. The times are simulated.
32 devices in a mesh: groups: 2 (over y), rows: 8 (over z, x), heads: 2 (over core).
Axes of the slice: x: 2, y: 2, z: 4, core: 2. Of those that a mesh axis runs over, the one named last changes fastest.
Arguments:
- residual_in: bfloat16 [128, 8192], P(('groups', 'rows'), 'heads'), parts along dimension 0, may hold values from -6 to 6
- query: bfloat16 [128, 8192], P(('groups', 'rows'), 'heads'), parts along dimension 0, may hold values from -120 to 120
- key_cache: bfloat16 [128, 4, 32, 128], P(('groups', 'rows'), 'heads'), parts along dimension 0, may hold values from -4 to 4
- value_cache: bfloat16 [128, 4, 32, 128], P(('groups', 'rows'), 'heads'), parts along dimension 0, may hold values from -5 to 5
- key_new: bfloat16 [128, 4, 128], P(('groups', 'rows'), 'heads'), parts along dimension 0, may hold values from -4 to 4
- value_new: bfloat16 [128, 4, 128], P(('groups', 'rows'), 'heads'), parts along dimension 0, may hold values from -5 to 5
- lengths: int32 [128], P(('groups', 'rows')), parts along dimension 0, may hold values from 2 to 32, as said below
- norm_gain: bfloat16 [8192], replicated, may hold values from 0.3984375 to 1.59375
- hot_gate: bfloat16 [128, 8192], P('heads'), may hold values from -0.0625 to 0.0625
- hot_up: bfloat16 [128, 8192], P('heads'), may hold values from -0.0625 to 0.0625
- hot_down: bfloat16 [128, 8192], P('heads'), may hold values from -0.5 to 0.5
- cold_gate: bfloat16 [512, 8192], P(('rows', 'heads')), may hold values from -0.0625 to 0.0625
- cold_up: bfloat16 [512, 8192], P(('rows', 'heads')), may hold values from -0.0625 to 0.0625
- cold_down: bfloat16 [512, 8192], P(('rows', 'heads')), may hold values from -0.5 to 0.5
- active: int32 [128, 4], P(('groups', 'rows')), parts along dimension 0, may hold values from 0 to 1, as said below
Outputs:
- residual_out: bfloat16 [128, 8192], P(('groups', 'rows'), 'heads'), parts along dimension 0
There are 2 independent parts, one for each index of `groups`. A program takes and returns all parts, laid end to end along the dimension named above; an argument that names none is the same for every part. Nothing has to cross between parts.
Inputs may be any that keep to these rules, and one draw needn't show every extreme that they name: `lengths`: every request has at least two filled slots, and some request has all 32. `active`: 0 or 1; among the 8 requests of one index of rows at most 2 are active on any one cold block, and exactly 2 on some.
All inputs are finite; a program needn't handle non-finite values.
Results may differ from a plain program's by a relative error of at most 0.0085.
Values may be sent and summed in bfloat16 or wider, within the bound.
No kernel may reach another device: no remote copies, remote signals or barrier semaphores. Data moves between devices by JAX's collectives and lax.ppermute only.
A program may use at most 64 MiB of HBM per device.

v0:
```python
import jax
import jax.numpy as jnp
from jax import lax
from jax.sharding import PartitionSpec as P

HD = 128
D = 8192
CAP = 2


def partner(block, axis, bit):
    count = lax.axis_size(axis)
    route = []
    for low in range(count):
        high = low | 1 << bit
        if high != low and high < count:
            route += [(low, high), (high, low)]
    return lax.ppermute(block, axis, route)


def join_halves(half, myself):
    other = partner(half, "heads", 0)
    low_first = jnp.concatenate([half, other], axis=1)
    high_first = jnp.concatenate([other, half], axis=1)
    return jnp.where(myself == 0, low_first, high_first)


def attention_rows(query, key_cache, value_cache, key_new, value_new, lengths):
    count = key_cache.shape[0]
    kv_local = key_cache.shape[1]
    scale_factor = 1.0 / HD**0.5
    queries = query.reshape(count, kv_local, -1, HD)
    scores = (
        jnp.einsum("rgjd,rgpd->rgjp", queries, key_cache, preferred_element_type=jnp.float32)
        * scale_factor
    )
    own_score = (
        jnp.einsum("rgjd,rgd->rgj", queries, key_new, preferred_element_type=jnp.float32)
        * scale_factor
    )
    visible = (jnp.arange(key_cache.shape[2], dtype=jnp.int32)[None, :] < lengths[:, None])[
        :, None, None, :
    ]
    scores = jnp.where(visible, scores, -1e30)
    highest = jnp.maximum(jnp.max(scores, axis=-1), own_score)
    expons = jnp.where(visible, jnp.exp(scores - highest[..., None]), 0.0)
    own_expon = jnp.exp(own_score - highest)
    totals = jnp.sum(expons, axis=-1) + own_expon
    weights = (expons / totals[..., None]).astype(jnp.bfloat16)
    own_weight = (own_expon / totals).astype(jnp.bfloat16)
    blended = jnp.einsum(
        "rgjp,rgpd->rgjd", weights, value_cache, preferred_element_type=jnp.float32
    )
    blended = (
        blended
        + own_weight.astype(jnp.float32)[..., None] * value_new.astype(jnp.float32)[:, :, None, :]
    )
    return blended.reshape(count, -1)


def swiglu_rows(normed, gate_rows, up_rows, down_rows):
    gate = jnp.einsum("rd,nd->rn", normed, gate_rows, preferred_element_type=jnp.float32)
    upper = jnp.einsum("rd,nd->rn", normed, up_rows, preferred_element_type=jnp.float32)
    hidden = (jax.nn.silu(gate) * upper).astype(jnp.bfloat16)
    return jnp.dot(hidden, down_rows, preferred_element_type=jnp.float32)


def collect_rows(selector, returned):
    return lax.dot_general(
        selector,
        returned,
        (((0,), (0,)), ((), ())),
        precision=lax.Precision.HIGHEST,
        preferred_element_type=jnp.float32,
    )


def local(
    residual_in,
    query,
    key_cache,
    value_cache,
    key_new,
    value_new,
    lengths,
    norm_gain,
    hot_gate,
    hot_up,
    hot_down,
    cold_gate,
    cold_up,
    cold_down,
    active,
):
    attended = attention_rows(query, key_cache, value_cache, key_new, value_new, lengths)
    stream = (residual_in.astype(jnp.float32) + attended).astype(jnp.bfloat16)
    half_width = stream.shape[1]
    myself = lax.axis_index("heads")
    local_wide = stream.astype(jnp.float32)
    square_part = jnp.sum(local_wide * local_wide, axis=-1)
    square_total = square_part + partner(square_part, "heads", 0)
    gain_half = lax.dynamic_slice_in_dim(norm_gain, myself * half_width, half_width)
    scaled = (
        local_wide * lax.rsqrt(square_total / D + 1e-05)[:, None] * gain_half.astype(jnp.float32)
    )
    normed = join_halves(scaled.astype(jnp.bfloat16), myself)
    hot_part = swiglu_rows(normed, hot_gate, hot_up, hot_down)
    owner_count = lax.axis_size("rows")
    block_count = active.shape[1]
    request_count = active.shape[0]
    by_block = jnp.transpose(active)
    earlier = jnp.cumsum(by_block, axis=1) - by_block
    slot_ids = jnp.arange(CAP, dtype=jnp.int32)[None, :, None]
    slot_table = by_block[:, None, :] * (earlier[:, None, :] == slot_ids).astype(jnp.int32)
    selector = jnp.repeat(slot_table, owner_count // block_count, axis=0).reshape(
        owner_count * CAP, request_count
    )
    outgoing = jnp.dot(
        selector.astype(jnp.bfloat16), normed, preferred_element_type=jnp.float32
    ).astype(jnp.bfloat16)
    incoming = lax.all_to_all(outgoing, "rows", split_axis=0, concat_axis=0, tiled=True)
    cold_part = swiglu_rows(incoming, cold_gate, cold_up, cold_down)
    selector_wide = selector.astype(jnp.float32)
    kept = lax.dynamic_slice_in_dim(cold_part, myself * half_width, half_width, 1)
    given = lax.dynamic_slice_in_dim(cold_part, (1 - myself) * half_width, half_width, 1)
    owner_sum = kept + partner(given, "heads", 0)
    returned = lax.all_to_all(owner_sum, "rows", split_axis=0, concat_axis=0, tiled=True)
    cold_sum = collect_rows(selector_wide, returned)
    hot_kept = lax.dynamic_slice_in_dim(hot_part, myself * half_width, half_width, 1)
    hot_given = lax.dynamic_slice_in_dim(hot_part, (1 - myself) * half_width, half_width, 1)
    hot_total = hot_kept + partner(hot_given, "heads", 0)
    result = stream.astype(jnp.float32) + hot_total + cold_sum
    return result.astype(jnp.bfloat16)


def solution(mesh):
    return jax.shard_map(
        local,
        mesh=mesh,
        in_specs=(
            P(("groups", "rows"), "heads"),
            P(("groups", "rows"), "heads"),
            P(("groups", "rows"), "heads", None, None),
            P(("groups", "rows"), "heads", None, None),
            P(("groups", "rows"), "heads", None),
            P(("groups", "rows"), "heads", None),
            P(("groups", "rows")),
            P(),
            P("heads", None),
            P("heads", None),
            P("heads", None),
            P(("rows", "heads"), None),
            P(("rows", "heads"), None),
            P(("rows", "heads"), None),
            P(("groups", "rows"), None),
        ),
        out_specs=P(("groups", "rows"), "heads"),
        check_vma=False,
    )
```

profile of v0, /device:TPU:0, one launch (start us, length us, event | category | flops | bytes accessed | tf_op | source)
XLA Modules:
  0.0 45.1 jit_solution(7972570449464875627)
XLA Ops:
  0.0 0.0 copy-start
  0.0 0.0 copy-start.4
  0.0 0.8 %iota_compare_fusion = pred[8,32]{1,0:T(8,128)(4,1)S(1)} fusion(s32[8]{0:T(128)} %param.21), kind=kLoop, calls=%fused_computation.44 | loop fusion | flops 256 | bytes 288 | tf_op jit(solution)/shard_map/lt | solution.py:41
  0.8 1.0 %fusion.14 = f32[8,2,1,16]{3,2,1,0:T(1,128)S(1)} fusion(bf16[8,2,16,128]{3,0,2,1:T(8,128)(2,1)} %bitcast.29, bf16[8,2,128,1]{2,1,0,3:T(2,128)(2,1)} %bitcast.37), kind=kOutput, calls=%fused_computation.26 | convolution fusion | flops 65536 | bytes 70656 | tf_op jit(solution)/shard_map/rgjd,rgd->rgj/dot_general | solution.py:38
  1.8 0.0 copy-done.4
  1.8 1.2 %fusion.36 = (f32[8,2,16]{2,1,0:T(2,128)S(1)}, f32[8,2,16,32]{3,2,1,0:T(8,128)S(1)}) fusion(bf16[8,2,32,128]{3,2,1,0:T(8,128)(2,1)} %param.17, bf16[8,2,16,128]{3,0,2,1:T(8,128)(2,1)S(1)} %bitcast.30, pred[8,32]{1,0:T(8,128)(4,1)S(1)} %iota_compare_fusion), kind=kOutput, calls=%fused_computation.58 | convolution fusion | flops 2121472 | bytes 230656 | tf_op jit(solution)/shard_map/rgjd,rgpd->rgjp/dot_general | solution.py:34
  3.0 0.0 copy-start.9
  3.0 0.2 fusion.9
  3.3 0.0 copy-start.8
  3.3 0.7 %copy-done.8 = bf16[8,2,128]{2,1,0:T(2,128)(2,1)S(1)} copy-done((bf16[8,2,128]{2,1,0:T(2,128)(2,1)S(1)}, bf16[8,2,128]{2,1,0:T(2,128)(2,1)}, u32[]{:S(2)}) %copy-start.8) | copy-done | bytes 4120
  4.0 0.0 copy-done.9
  4.0 0.0 copy-start.5
  4.0 0.0 copy-start.6
  4.0 0.3 convolution_add_fusion
  4.2 0.0 copy-start.7
  4.2 0.5 %copy-done.5 = bf16[8,4096]{1,0:T(8,128)(2,1)S(1)} copy-done((bf16[8,4096]{1,0:T(8,128)(2,1)S(1)}, bf16[8,4096]{1,0:T(8,128)(2,1)}, u32[]{:S(2)}) %copy-start.5) | copy-done | bytes 65560
  4.8 0.0 copy-start.1
  4.8 0.2 fusion.3
  5.0 0.5 %collective-permute-start = (f32[8]{0:T(128)S(1)}, f32[8]{0:T(128)S(1)}, u32[]{:S(2)}, u32[]{:S(2)}) collective-permute-start(f32[8]{0:T(128)S(1)} %get-tuple-element.5), channel_id=1, source_target_pairs={{0,1},{1,0},{2,3},{3,2},{4,5},{5,4},{6,7},{7,6},{8,9},{9,8},{10,11... | collective-permute-start | bytes 104 | tf_op jit(solution)/shard_map/ppermute | solution.py:18
  5.5 0.0 copy-done.6
  5.5 0.2 reduce_window_sum.11
  5.7 0.0 copy-done.7
  5.7 0.6 %collective-permute-done = f32[8]{0:T(128)S(1)} collective-permute-done((f32[8]{0:T(128)S(1)}, f32[8]{0:T(128)S(1)}, u32[]{:S(2)}, u32[]{:S(2)}) %collective-permute-start) | collective-permute-done | bytes 64 | tf_op jit(solution)/shard_map/ppermute | solution.py:18
  6.3 0.1 fusion.5
  6.4 0.4 collective-permute-start.1
  6.8 0.9 %collective-permute-done.1 = bf16[8,4096]{1,0:T(8,128)(2,1)S(1)} collective-permute-done((bf16[8,4096]{1,0:T(8,128)(2,1)S(1)}, bf16[8,4096]{1,0:T(8,128)(2,1)S(1)}, u32[]{:S(2)}, u32[]{:S(2)}) %collective-permute-start.1) | collective-permute-done | bytes 65568 | tf_op jit(solution)/shard_map/ppermute | solution.py:18
  7.7 0.2 convolution_convert_fusion
  8.0 0.9 %all_to_all.16 = bf16[8,2,8192]{2,1,0:T(2,128)(2,1)} reshape(bf16[16,8192]{1,0:T(8,128)(2,1)S(1)} %convolution_convert_fusion) | data formatting | bytes 524288 | tf_op jit(solution)/shard_map/all_to_all | solution.py:121
  8.9 7.1 %all-to-all-start = ((bf16[8,2,8192]{2,1,0:T(2,128)(2,1)}), bf16[8,2,8192]{2,1,0:T(2,128)(2,1)S(1)}, u32[]{:S(2)}, u32[]{:S(2)}) async-start(bf16[8,2,8192]{2,1,0:T(2,128)(2,1)} %all_to_all.16), calls=%async_computation | async-start | bytes 524288 | tf_op jit(solution)/shard_map/all_to_all | solution.py:121
  16.0 0.0 copy-done.1
  16.0 0.4 fusion.33
  16.3 0.0 copy-start.3
  16.3 8.9 %all-to-all-done = bf16[8,2,8192]{2,1,0:T(2,128)(2,1)S(1)} async-done(((bf16[8,2,8192]{2,1,0:T(2,128)(2,1)}), bf16[8,2,8192]{2,1,0:T(2,128)(2,1)S(1)}, u32[]{:S(2)}, u32[]{:S(2)}) %all-to-all-start) | async-done | bytes 262176 | tf_op jit(solution)/shard_map/all_to_all | solution.py:121
  25.3 0.1 all_to_all.18
  25.4 0.0 copy-done.3
  25.4 0.2 fusion.37
  25.6 0.0 copy-start.2
  25.6 1.9 %fusion.2 = f32[16,8192]{1,0:T(8,128)S(1)} fusion(bf16[32,8192]{1,0:T(8,128)(2,1)} %param.28, bf16[16,8192]{1,0:T(8,128)(2,1)S(1)} %all_to_all.18, bf16[32,8192]{1,0:T(8,128)(2,1)} %param.27, f32[16,32]{1,0:T(8,128)S(1)} %fusion.37), kind=kOutput, calls=%fused_computation.6 | convolution fusion | flops 16780288 | bytes 1837056 | tf_op jit(solution)/shard_map/dot_general | solution.py:65
  27.5 0.1 collective-permute-start.3
  27.6 0.0 copy-done
  27.6 0.0 copy-done.2
  27.6 0.9 %fusion.27 = f32[8,8192]{1,0:T(8,128)S(1)} fusion(bf16[64,8192]{1,0:T(8,128)(2,1)S(1)} %copy-done, f32[8,64]{1,0:T(8,128)S(1)} %fusion.33, bf16[64,8192]{1,0:T(8,128)(2,1)S(1)} %copy-done.2, bf16[8,4096]{1,0:T(8,128)(2,1)S(1)} %collective-permute-done.1, bf16[8,4096]{1,0:T(8,128)(2,1)S(1)} %fusion.5, pred[]{:T(512)S(6)} %eq.16), kind=kOutput, calls=%fused_computation.46 | convolution fusion | flops 17370112 | bytes 2492417 | tf_op jit(solution)/shard_map/dot_general | solution.py:65
  28.5 0.7 %collective-permute-done.3 = f32[16,4096]{1,0:T(8,128)} collective-permute-done((f32[16,4096]{1,0:T(8,128)S(1)}, f32[16,4096]{1,0:T(8,128)}, u32[]{:S(2)}, u32[]{:S(2)}) %collective-permute-start.3) | collective-permute-done | bytes 262176 | tf_op jit(solution)/shard_map/ppermute | solution.py:18
  29.3 1.0 %dynamic-slice_add_fusion = f32[16,4096]{1,0:T(8,128)S(1)} fusion(f32[16,4096]{1,0:T(8,128)} %collective-permute-done.3, f32[16,8192]{1,0:T(8,128)S(1)} %fusion.2, s32[]{:T(128)S(6)} %select_n.27), kind=kLoop, calls=%fused_computation.7 | loop fusion | flops 65536 | bytes 786436 | tf_op jit(solution)/shard_map/add | solution.py:126
  30.2 0.9 %all_to_all.19 = f32[8,2,4096]{2,1,0:T(2,128)} reshape(f32[16,4096]{1,0:T(8,128)S(1)} %dynamic-slice_add_fusion) | data formatting | bytes 524288 | tf_op jit(solution)/shard_map/all_to_all | solution.py:127
  31.1 3.6 %all-to-all-start.1 = ((f32[8,2,4096]{2,1,0:T(2,128)}), f32[8,2,4096]{2,1,0:T(2,128)S(1)}, u32[]{:S(2)}, u32[]{:S(2)}) async-start(f32[8,2,4096]{2,1,0:T(2,128)} %all_to_all.19), calls=%async_computation.1 | async-start | bytes 524288 | tf_op jit(solution)/shard_map/all_to_all | solution.py:127
  34.7 0.1 collective-permute-start.2
  34.8 9.2 %all-to-all-done.1 = f32[8,2,4096]{2,1,0:T(2,128)S(1)} async-done(((f32[8,2,4096]{2,1,0:T(2,128)}), f32[8,2,4096]{2,1,0:T(2,128)S(1)}, u32[]{:S(2)}, u32[]{:S(2)}) %all-to-all-start.1) | async-done | bytes 262176 | tf_op jit(solution)/shard_map/all_to_all | solution.py:127
  44.0 0.2 all_to_all.21
  44.1 0.0 collective-permute-done.2
  44.2 1.0 %fusion.7 = bf16[8,4096]{1,0:T(8,128)(2,1)} fusion(bf16[8,4096]{1,0:T(8,128)(2,1)S(1)} %get-tuple-element.6, f32[8,4096]{1,0:T(8,128)S(1)} %collective-permute-done.2, f32[8,8192]{1,0:T(8,128)S(1)} %fusion.27, s32[]{:T(128)S(6)} %select_n.27, f32[16,8]{1,0:T(8,128)S(1)} %bitcast.31, f32[16,4096]{1,0:T(8,128)S(1)} %all_to_all.21), kind=kOutput, calls=%fused_computation.15 | convolution fusion | flops 6455296 | bytes 655876 | tf_op jit(solution)/shard_map/dot_general | solution.py:69
  (11 shorter events, 0.1 us)
Async XLA Ops:
  0.0 27.6 %copy-start = (bf16[64,8192]{1,0:T(8,128)(2,1)S(1)}, bf16[64,8192]{1,0:T(8,128)(2,1)}, u32[]{:S(2)}) copy-start(bf16[64,8192]{1,0:T(8,128)(2,1)} %param.25) | copy-start | bytes 3145732
  0.0 1.8 %copy-start.4 = (bf16[8,4096]{1,0:T(8,128)(2,1)S(1)}, bf16[8,4096]{1,0:T(8,128)(2,1)}, u32[]{:S(2)}) copy-start(bf16[8,4096]{1,0:T(8,128)(2,1)} %param.16) | copy-start | bytes 196612
  3.0 1.0 %copy-start.9 = (bf16[8,2,32,128]{3,2,1,0:T(8,128)(2,1)S(1)}, bf16[8,2,32,128]{3,2,1,0:T(8,128)(2,1)}, u32[]{:S(2)}) copy-start(bf16[8,2,32,128]{3,2,1,0:T(8,128)(2,1)} %param.18) | copy-start | bytes 393220
  3.3 0.7 %copy-start.8 = (bf16[8,2,128]{2,1,0:T(2,128)(2,1)S(1)}, bf16[8,2,128]{2,1,0:T(2,128)(2,1)}, u32[]{:S(2)}) copy-start(bf16[8,2,128]{2,1,0:T(2,128)(2,1)} %param.20) | copy-start | bytes 12292
  4.0 0.8 %copy-start.5 = (bf16[8,4096]{1,0:T(8,128)(2,1)S(1)}, bf16[8,4096]{1,0:T(8,128)(2,1)}, u32[]{:S(2)}) copy-start(bf16[8,4096]{1,0:T(8,128)(2,1)} %param.15) | copy-start | bytes 196612
  4.0 1.5 %copy-start.6 = (s32[8,4]{0,1:T(4,128)S(1)}, s32[8,4]{0,1:T(4,128)}, u32[]{:S(2)}) copy-start(s32[8,4]{0,1:T(4,128)} %param.29) | copy-start | bytes 388
  4.2 1.5 %copy-start.7 = (bf16[8192]{0:T(1024)(128)(2,1)S(1)}, bf16[8192]{0:T(1024)(128)(2,1)}, u32[]{:S(2)}) copy-start(bf16[8192]{0:T(1024)(128)(2,1)} %param.22) | copy-start | bytes 49156
  4.8 11.2 %copy-start.1 = (bf16[64,8192]{1,0:T(8,128)(2,1)S(1)}, bf16[64,8192]{1,0:T(8,128)(2,1)}, u32[]{:S(2)}) copy-start(bf16[64,8192]{1,0:T(8,128)(2,1)} %param.24) | copy-start | bytes 3145732
  5.0 1.3 %collective-permute-start = (f32[8]{0:T(128)S(1)}, f32[8]{0:T(128)S(1)}, u32[]{:S(2)}, u32[]{:S(2)}) collective-permute-start(f32[8]{0:T(128)S(1)} %get-tuple-element.5), channel_id=1, source_target_pairs={{0,1},{1,0},{2,3},{3,2},{4,5},{5,4},{6,7},{7,6},{8,9},{9,8},{10,11... | collective-permute-start | bytes 104 | tf_op jit(solution)/shard_map/ppermute | solution.py:18
  6.4 1.3 %collective-permute-start.1 = (bf16[8,4096]{1,0:T(8,128)(2,1)S(1)}, bf16[8,4096]{1,0:T(8,128)(2,1)S(1)}, u32[]{:S(2)}, u32[]{:S(2)}) collective-permute-start(bf16[8,4096]{1,0:T(8,128)(2,1)S(1)} %fusion.5), channel_id=1, source_target_pairs={{0,1},{1,0},{2,3},{3,2},{4,5},{5,4},{6,7},{7,6},{8,9},{9,8},{10,11... | collective-permute-start | bytes 196616 | tf_op jit(solution)/shard_map/ppermute | solution.py:18
  8.9 16.4 %all-to-all-start = ((bf16[8,2,8192]{2,1,0:T(2,128)(2,1)}), bf16[8,2,8192]{2,1,0:T(2,128)(2,1)S(1)}, u32[]{:S(2)}, u32[]{:S(2)}) async-start(bf16[8,2,8192]{2,1,0:T(2,128)(2,1)} %all_to_all.16), calls=%async_computation | async-start | bytes 524288 | tf_op jit(solution)/shard_map/all_to_all | solution.py:121
  16.3 9.0 %copy-start.3 = (bf16[32,8192]{1,0:T(8,128)(2,1)S(1)}, bf16[32,8192]{1,0:T(8,128)(2,1)}, u32[]{:S(2)}) copy-start(bf16[32,8192]{1,0:T(8,128)(2,1)} %param.26) | copy-start | bytes 1572868
  25.6 2.0 %copy-start.2 = (bf16[64,8192]{1,0:T(8,128)(2,1)S(1)}, bf16[64,8192]{1,0:T(8,128)(2,1)}, u32[]{:S(2)}) copy-start(bf16[64,8192]{1,0:T(8,128)(2,1)} %param.23) | copy-start | bytes 3145732
  27.5 1.7 %collective-permute-start.3 = (f32[16,4096]{1,0:T(8,128)S(1)}, f32[16,4096]{1,0:T(8,128)}, u32[]{:S(2)}, u32[]{:S(2)}) collective-permute-start(f32[16,4096]{1,0:T(8,128)S(1)} %constant_dynamic-slice_fusion), channel_id=1, source_target_pairs={{0,1},{1,0},{2,3},{3,2},{4,5},{5,4},{6,7},{7,6},{8,9},{9,8},{10,11... | collective-permute-start | bytes 786440 | tf_op jit(solution)/shard_map/ppermute | solution.py:18
  31.1 12.9 %all-to-all-start.1 = ((f32[8,2,4096]{2,1,0:T(2,128)}), f32[8,2,4096]{2,1,0:T(2,128)S(1)}, u32[]{:S(2)}, u32[]{:S(2)}) async-start(f32[8,2,4096]{2,1,0:T(2,128)} %all_to_all.19), calls=%async_computation.1 | async-start | bytes 524288 | tf_op jit(solution)/shard_map/all_to_all | solution.py:127
  34.7 9.4 %collective-permute-start.2 = (f32[8,4096]{1,0:T(8,128)S(1)}, f32[8,4096]{1,0:T(8,128)S(1)}, u32[]{:S(2)}, u32[]{:S(2)}) collective-permute-start(f32[8,4096]{1,0:T(8,128)S(1)} %constant_dynamic-slice_fusion.1), channel_id=1, source_target_pairs={{0,1},{1,0},{2,3},{3,2},{4,5},{5,4},{6,7},{7,6},{8,9},{9,8},{10,11... | collective-permute-start | bytes 393224 | tf_op jit(solution)/shard_map/ppermute | solution.py:18
where the time goes:
time: 45.6 us; the launch traced here: 45.1 us
  waiting for transfers between devices  20.4 us (45%)
  starting transfers between devices  11.7 us (26%)
  matrix products  6.98 us (15%)
  local copies, waits for them, and re-layouts  3.33 us (7%)
  other arithmetic  2.53 us (6%)
    all_to_all x1, waiting for transfers between devices, local(): lax.all_to_all(owner_sum, 'rows', split_axis=0, concat_axis=0, tiled=True)  9.17 us
    all_to_all x1, waiting for transfers between devices, local(): lax.all_to_all(outgoing, 'rows', split_axis=0, concat_axis=0, tiled=True)  8.91 us
    all_to_all x1, starting transfers between devices, local(): lax.all_to_all(outgoing, 'rows', split_axis=0, concat_axis=0, tiled=True)  7.1 us
    all_to_all x1, starting transfers between devices, local(): lax.all_to_all(owner_sum, 'rows', split_axis=0, concat_axis=0, tiled=True)  3.59 us
    dot_general x2, matrix products, swiglu_rows(): return jnp.dot(hidden, down_rows, preferred_element_type=jnp.float32)  2.78 us
    ppermute x4, waiting for transfers between devices, partner(): return lax.ppermute(block, axis, route)  2.3 us
    unnamed x20, local copies, waits for them, and re-layouts  1.24 us
    dot_general x1, matrix products, attention_rows(): jnp.einsum('rgjd,rgpd->rgjp', queries, key_cache, preferred_element_type=...  1.17 us
  transfers between devices with their start and end apart: 6, of which 5 were waited for; matrix products, arithmetic and copies ran while one was open for 3% of the time, Pallas kernels for 0%

commit v1 on v0

--- a/solution.py
+++ b/solution.py
@@ -6,6 +6,18 @@
 HD = 128
 D = 8192
 CAP = 2
+
+
+def split_up(x, dim, size):
+    dims = x.shape
+    blocks = x.reshape(*dims[:dim], size, dims[dim] // size, *dims[dim + 1 :])
+    return jnp.moveaxis(blocks, dim, 0)
+
+
+def joined_along(blocks, dim):
+    blocks = jnp.moveaxis(blocks, 0, dim)
+    dims = blocks.shape
+    return blocks.reshape(*dims[:dim], dims[dim] * dims[dim + 1], *dims[dim + 2 :])
 
 
 def partner(block, axis, bit):
@@ -124,7 +136,15 @@
     kept = lax.dynamic_slice_in_dim(cold_part, myself * half_width, half_width, 1)
     given = lax.dynamic_slice_in_dim(cold_part, (1 - myself) * half_width, half_width, 1)
     owner_sum = kept + partner(given, "heads", 0)
-    returned = lax.all_to_all(owner_sum, "rows", split_axis=0, concat_axis=0, tiled=True)
+    length, index = (lax.axis_size("rows"), lax.axis_index("rows"))
+    blocks = split_up(owner_sum, 0, length)
+    filled = blocks
+    for hop in range(1, length):
+        target, source = ((index + hop) % length, (index - hop) % length)
+        sent = lax.dynamic_index_in_dim(blocks, target, 0)
+        received = lax.ppermute(sent, "rows", [(i, (i + hop) % length) for i in range(length)])
+        filled = lax.dynamic_update_slice_in_dim(filled, received, source, axis=0)
+    returned = joined_along(filled, 0)
     cold_sum = collect_rows(selector_wide, returned)
     hot_kept = lax.dynamic_slice_in_dim(hot_part, myself * half_width, half_width, 1)
     hot_given = lax.dynamic_slice_in_dim(hot_part, (1 - myself) * half_width, half_width, 1)

time: 45.6 us -> 50.8 us (1.11)
  starting transfers between devices: 11.7 us -> 16 us
  local copies, waits for them, and re-layouts: 3.33 us -> 5.36 us
  other arithmetic: 2.53 us -> 1.58 us
    ppermute x0 -> x7, waiting for transfers between devices: none -> 9.54 us  [local(): lax.ppermute(sent, 'rows', [(i, (i + hop) % length) for i in range(length)])]
    all_to_all x1 -> x0, waiting for transfers between devices: 9.17 us -> none  [local(): lax.all_to_all(owner_sum, 'rows', split_axis=0, concat_axis=0, tiled=True)]
    ppermute x0 -> x7, starting transfers between devices: none -> 7.84 us  [local(): lax.ppermute(sent, 'rows', [(i, (i + hop) % length) for i in range(length)])]
    all_to_all x1 -> x0, starting transfers between devices: 3.59 us -> none  [local(): lax.all_to_all(owner_sum, 'rows', split_axis=0, concat_axis=0, tiled=True)]
    unnamed x20 -> x26, local copies, waits for them, and re-layouts: 1.24 us -> 3.85 us
    ppermute x4, waiting for transfers between devices: 2.3 us -> 1.19 us  [partner(): return lax.ppermute(block, axis, route)]
    all_to_all x2 -> x0, local copies, waits for them, and re-layouts: 1.04 us -> none  [local(): lax.all_to_all(owner_sum, 'rows', split_axis=0, concat_axis=0, tiled=True)]
    add x1, other arithmetic: 0.98 us -> 0.03 us  [local(): owner_sum = kept + partner(given, 'heads', 0)]
  transfers between devices with their start and end apart: 6 -> 12, of which waited for: 5 -> 7; matrix products, arithmetic and copies ran while one was open for 3% -> 3% of each run, Pallas kernels for 0% -> 0%
where the time goes in v1:
time: 50.8 us; the launch traced here: 50.3 us
  waiting for transfers between devices  20.1 us (40%)
  starting transfers between devices  16 us (31%)
  matrix products  6.79 us (13%)
  local copies, waits for them, and re-layouts  5.36 us (11%)
  other arithmetic  1.58 us (3%)
    ppermute x7, waiting for transfers between devices, local(): lax.ppermute(sent, 'rows', [(i, (i + hop) % length) for i in range(length)])  9.54 us
    all_to_all x1, waiting for transfers between devices, local(): lax.all_to_all(outgoing, 'rows', split_axis=0, concat_axis=0, tiled=True)  9.36 us
    ppermute x7, starting transfers between devices, local(): lax.ppermute(sent, 'rows', [(i, (i + hop) % length) for i in range(length)])  7.84 us
    all_to_all x1, starting transfers between devices, local(): lax.all_to_all(outgoing, 'rows', split_axis=0, concat_axis=0, tiled=True)  7.17 us
    unnamed x26, local copies, waits for them, and re-layouts  3.85 us
    dot_general x2, matrix products, swiglu_rows(): return jnp.dot(hidden, down_rows, preferred_element_type=jnp.float32)  2.6 us
    ppermute x4, waiting for transfers between devices, partner(): return lax.ppermute(block, axis, route)  1.19 us
    dot_general x1, matrix products, attention_rows(): jnp.einsum('rgjd,rgpd->rgjp', queries, key_cache, preferred_element_type=...  1.17 us
  transfers between devices with their start and end apart: 12, of which 7 were waited for; matrix products, arithmetic and copies ran while one was open for 3% of the time, Pallas kernels for 0%

profile of v1, /device:TPU:0, one launch (start us, length us, event | category | flops | bytes accessed | tf_op | source)
XLA Modules:
  0.0 50.3 jit_solution(10169091310900609631)
XLA Ops:
  0.0 0.0 copy-start
  0.0 0.0 copy-start.7
  0.0 0.8 %iota_compare_fusion = pred[8,32]{1,0:T(8,128)(4,1)S(1)} fusion(s32[8]{0:T(128)} %param.21), kind=kLoop, calls=%fused_computation.60 | loop fusion | flops 256 | bytes 288 | tf_op jit(solution)/shard_map/lt | solution.py:53
  0.8 1.0 %fusion.14 = f32[8,2,1,16]{3,2,1,0:T(1,128)S(1)} fusion(bf16[8,2,16,128]{3,0,2,1:T(8,128)(2,1)} %bitcast.29, bf16[8,2,128,1]{2,1,0,3:T(2,128)(2,1)} %bitcast.37), kind=kOutput, calls=%fused_computation.26 | convolution fusion | flops 65536 | bytes 70656 | tf_op jit(solution)/shard_map/rgjd,rgd->rgj/dot_general | solution.py:50
  1.8 0.0 copy-done.7
  1.8 1.2 %fusion.36 = (f32[8,2,16]{2,1,0:T(2,128)S(1)}, f32[8,2,16,32]{3,2,1,0:T(8,128)S(1)}) fusion(bf16[8,2,32,128]{3,2,1,0:T(8,128)(2,1)} %param.17, bf16[8,2,16,128]{3,0,2,1:T(8,128)(2,1)S(1)} %bitcast.30, pred[8,32]{1,0:T(8,128)(4,1)S(1)} %iota_compare_fusion), kind=kOutput, calls=%fused_computation.72 | convolution fusion | flops 2121472 | bytes 230656 | tf_op jit(solution)/shard_map/rgjd,rgpd->rgjp/dot_general | solution.py:46
  3.0 0.0 copy-start.12
  3.0 0.2 fusion.9
  3.3 0.0 copy-start.11
  3.3 0.7 %copy-done.11 = bf16[8,2,128]{2,1,0:T(2,128)(2,1)S(1)} copy-done((bf16[8,2,128]{2,1,0:T(2,128)(2,1)S(1)}, bf16[8,2,128]{2,1,0:T(2,128)(2,1)}, u32[]{:S(2)}) %copy-start.11) | copy-done | bytes 4120
  4.0 0.0 copy-done.12
  4.0 0.0 copy-start.8
  4.0 0.3 convolution_add_fusion
  4.2 0.6 %copy-done.8 = bf16[8,4096]{1,0:T(8,128)(2,1)S(1)} copy-done((bf16[8,4096]{1,0:T(8,128)(2,1)S(1)}, bf16[8,4096]{1,0:T(8,128)(2,1)}, u32[]{:S(2)}) %copy-start.8) | copy-done | bytes 65560
  4.8 0.0 copy-start.10
  4.8 0.2 fusion.3
  5.0 0.5 %collective-permute-start = (f32[8]{0:T(128)S(1)}, f32[8]{0:T(128)S(1)}, u32[]{:S(2)}, u32[]{:S(2)}) collective-permute-start(f32[8]{0:T(128)S(1)} %get-tuple-element.5), channel_id=1, source_target_pairs={{0,1},{1,0},{2,3},{3,2},{4,5},{5,4},{6,7},{7,6},{8,9},{9,8},{10,11... | collective-permute-start | bytes 104 | tf_op jit(solution)/shard_map/ppermute | solution.py:30
  5.5 0.7 %copy-done.9 = s32[8,4]{0,1:T(4,128)S(1)} copy-done((s32[8,4]{0,1:T(4,128)S(1)}, s32[8,4]{0,1:T(4,128)}, u32[]{:S(2)}) %copy-start.9) | copy-done | bytes 152
  6.2 0.2 reduce_window_sum.11
  6.4 0.0 copy-done.10
  6.4 0.0 collective-permute-done
  6.4 0.1 fusion.5
  6.5 0.3 collective-permute-start.1
  6.8 1.0 %collective-permute-done.1 = bf16[8,4096]{1,0:T(8,128)(2,1)S(1)} collective-permute-done((bf16[8,4096]{1,0:T(8,128)(2,1)S(1)}, bf16[8,4096]{1,0:T(8,128)(2,1)S(1)}, u32[]{:S(2)}, u32[]{:S(2)}) %collective-permute-start.1) | collective-permute-done | bytes 65568 | tf_op jit(solution)/shard_map/ppermute | solution.py:30
  7.8 0.2 convolution_convert_fusion
  8.0 0.4 copy-done.5
  8.4 0.9 %all_to_all.8 = bf16[8,2,8192]{2,1,0:T(2,128)(2,1)} reshape(bf16[16,8192]{1,0:T(8,128)(2,1)S(1)} %convolution_convert_fusion) | data formatting | bytes 524288 | tf_op jit(solution)/shard_map/all_to_all | solution.py:133
  9.3 7.2 %all-to-all-start = ((bf16[8,2,8192]{2,1,0:T(2,128)(2,1)}), bf16[8,2,8192]{2,1,0:T(2,128)(2,1)S(1)}, u32[]{:S(2)}, u32[]{:S(2)}) async-start(bf16[8,2,8192]{2,1,0:T(2,128)(2,1)} %all_to_all.8), calls=%async_computation | async-start | bytes 524288 | tf_op jit(solution)/shard_map/all_to_all | solution.py:133
  16.5 9.4 %all-to-all-done = bf16[8,2,8192]{2,1,0:T(2,128)(2,1)S(1)} async-done(((bf16[8,2,8192]{2,1,0:T(2,128)(2,1)}), bf16[8,2,8192]{2,1,0:T(2,128)(2,1)S(1)}, u32[]{:S(2)}, u32[]{:S(2)}) %all-to-all-start) | async-done | bytes 262176 | tf_op jit(solution)/shard_map/all_to_all | solution.py:133
  25.8 0.1 all_to_all.10
  25.9 0.0 copy-done.4
  26.0 0.0 copy-start.3
  26.0 0.2 fusion.37
  26.2 0.8 %copy-done.3 = bf16[32,8192]{1,0:T(8,128)(2,1)S(1)} copy-done((bf16[32,8192]{1,0:T(8,128)(2,1)S(1)}, bf16[32,8192]{1,0:T(8,128)(2,1)}, u32[]{:S(2)}) %copy-start.3) | copy-done | bytes 524312
  27.0 1.7 %fusion.2 = f32[16,8192]{1,0:T(8,128)S(1)} fusion(bf16[32,8192]{1,0:T(8,128)(2,1)S(1)} %copy-done.3, bf16[16,8192]{1,0:T(8,128)(2,1)S(1)} %all_to_all.10, bf16[32,8192]{1,0:T(8,128)(2,1)} %param.27, f32[16,32]{1,0:T(8,128)S(1)} %fusion.37), kind=kOutput, calls=%fused_computation.6 | convolution fusion | flops 16780288 | bytes 1837056 | tf_op jit(solution)/shard_map/dot_general | solution.py:77
  28.7 0.1 collective-permute-start.3
  28.9 0.0 copy-start.6
  29.1 0.0 copy-done.1
  29.1 0.7 %copy-done.6 = bf16[8,4096]{1,0:T(8,128)(2,1)S(1)} copy-done((bf16[8,4096]{1,0:T(8,128)(2,1)S(1)}, bf16[8,4096]{1,0:T(8,128)(2,1)}, u32[]{:S(2)}) %copy-start.6) | copy-done | bytes 65560
  29.8 0.4 fusion.33
  30.2 0.2 collective-permute-done.3
  30.4 0.2 reshape.43
  30.5 1.5 %collective-permute-start.4 = (f32[1,2,4096]{2,1,0:T(2,128)S(1)}, f32[1,2,4096]{2,1,0:T(2,128)S(1)}, u32[]{:S(2)}, u32[]{:S(2)}) collective-permute-start(f32[1,2,4096]{2,1,0:T(2,128)S(1)} %constant_dynamic-slice_fusion.6), channel_id=1, source_target_pairs={{0,2},{2,4},{4,6},{6,8},{8,10},{10,12},{12,14},{14,0},{1,3},{3,5},... | collective-permute-start | bytes 98312 | tf_op jit(solution)/shard_map/ppermute | solution.py:145
  32.0 0.0 copy-done
  32.0 0.0 copy-done.2
  32.0 0.9 %fusion.27 = f32[8,8192]{1,0:T(8,128)S(1)} fusion(bf16[64,8192]{1,0:T(8,128)(2,1)S(1)} %copy-done, f32[8,64]{1,0:T(8,128)S(1)} %fusion.33, bf16[64,8192]{1,0:T(8,128)(2,1)S(1)} %copy-done.2, bf16[8,4096]{1,0:T(8,128)(2,1)S(1)} %copy-done.6, bf16[8,4096]{1,0:T(8,128)(2,1)S(1)} %fusion.5, pred[]{:T(512)S(6)} %eq.31), kind=kOutput, calls=%fused_computation.62 | convolution fusion | flops 17370112 | bytes 2492417 | tf_op jit(solution)/shard_map/dot_general | solution.py:77
  32.9 4.3 %collective-permute-done.4 = f32[1,2,4096]{2,1,0:T(2,128)S(1)} collective-permute-done((f32[1,2,4096]{2,1,0:T(2,128)S(1)}, f32[1,2,4096]{2,1,0:T(2,128)S(1)}, u32[]{:S(2)}, u32[]{:S(2)}) %collective-permute-start.4) | collective-permute-done | bytes 32800 | tf_op jit(solution)/shard_map/ppermute | solution.py:145
  37.2 0.1 constant_dynamic-slice_fusion
  37.3 0.1 collective-permute-start.5
  37.4 0.1 collective-permute-start.2
  37.5 0.1 collective-permute-start.6
  37.5 2.5 %collective-permute-start.7 = (f32[1,2,4096]{2,1,0:T(2,128)S(1)}, f32[1,2,4096]{2,1,0:T(2,128)S(1)}, u32[]{:S(2)}, u32[]{:S(2)}) collective-permute-start(f32[1,2,4096]{2,1,0:T(2,128)S(1)} %get-tuple-element.10), channel_id=1, source_target_pairs={{0,8},{2,10},{4,12},{6,14},{8,0},{10,2},{12,4},{14,6},{1,9},{3,11}... | collective-permute-start | bytes 98312 | tf_op jit(solution)/shard_map/ppermute | solution.py:145
  40.0 1.3 %collective-permute-start.8 = (f32[1,2,4096]{2,1,0:T(2,128)S(1)}, f32[1,2,4096]{2,1,0:T(2,128)S(1)}, u32[]{:S(2)}, u32[]{:S(2)}) collective-permute-start(f32[1,2,4096]{2,1,0:T(2,128)S(1)} %get-tuple-element.9), channel_id=1, source_target_pairs={{0,10},{2,12},{4,14},{6,0},{8,2},{10,4},{12,6},{14,8},{1,11},{3,13... | collective-permute-start | bytes 98312 | tf_op jit(solution)/shard_map/ppermute | solution.py:145
  41.3 2.1 %collective-permute-done.5 = f32[1,2,4096]{2,1,0:T(2,128)S(1)} collective-permute-done((f32[1,2,4096]{2,1,0:T(2,128)S(1)}, f32[1,2,4096]{2,1,0:T(2,128)S(1)}, u32[]{:S(2)}, u32[]{:S(2)}) %collective-permute-start.5) | collective-permute-done | bytes 32800 | tf_op jit(solution)/shard_map/ppermute | solution.py:145
  43.4 1.7 %collective-permute-start.9 = (f32[1,2,4096]{2,1,0:T(2,128)S(1)}, f32[1,2,4096]{2,1,0:T(2,128)S(1)}, u32[]{:S(2)}, u32[]{:S(2)}) collective-permute-start(f32[1,2,4096]{2,1,0:T(2,128)S(1)} %get-tuple-element.8), channel_id=1, source_target_pairs={{0,12},{2,14},{4,0},{6,2},{8,4},{10,6},{12,8},{14,10},{1,13},{3,15... | collective-permute-start | bytes 98312 | tf_op jit(solution)/shard_map/ppermute | solution.py:145
  45.2 0.0 collective-permute-done.6
  45.2 0.7 %collective-permute-start.10 = (f32[1,2,4096]{2,1,0:T(2,128)S(1)}, f32[1,2,4096]{2,1,0:T(2,128)S(1)}, u32[]{:S(2)}, u32[]{:S(2)}) collective-permute-start(f32[1,2,4096]{2,1,0:T(2,128)S(1)} %get-tuple-element.7), channel_id=1, source_target_pairs={{0,14},{2,0},{4,2},{6,4},{8,6},{10,8},{12,10},{14,12},{1,15},{3,1}... | collective-permute-start | bytes 98312 | tf_op jit(solution)/shard_map/ppermute | solution.py:145
  45.9 0.0 collective-permute-done.7
  45.9 0.0 collective-permute-done.8
  45.9 1.9 %collective-permute-done.9 = f32[1,2,4096]{2,1,0:T(2,128)S(1)} collective-permute-done((f32[1,2,4096]{2,1,0:T(2,128)S(1)}, f32[1,2,4096]{2,1,0:T(2,128)S(1)}, u32[]{:S(2)}, u32[]{:S(2)}) %collective-permute-start.9) | collective-permute-done | bytes 32800 | tf_op jit(solution)/shard_map/ppermute | solution.py:145
  47.8 1.3 %collective-permute-done.10 = f32[1,2,4096]{2,1,0:T(2,128)S(1)} collective-permute-done((f32[1,2,4096]{2,1,0:T(2,128)S(1)}, f32[1,2,4096]{2,1,0:T(2,128)S(1)}, u32[]{:S(2)}, u32[]{:S(2)}) %collective-permute-start.10) | collective-permute-done | bytes 32800 | tf_op jit(solution)/shard_map/ppermute | solution.py:145
  49.1 0.2 reshape.44
  49.3 0.0 collective-permute-done.2
  49.3 1.0 %fusion.7 = bf16[8,4096]{1,0:T(8,128)(2,1)} fusion(bf16[8,4096]{1,0:T(8,128)(2,1)S(1)} %get-tuple-element.6, f32[8,4096]{1,0:T(8,128)S(1)} %collective-permute-done.2, f32[8,8192]{1,0:T(8,128)S(1)} %fusion.27, s32[]{:T(128)S(6)} %select_n.129, f32[16,8]{1,0:T(8,128)S(1)} %bitcast.31, f32[16,4096]{1,0:T(8,128)S(1)} %reshape.44), kind=kOutput, calls=%fused_computation.15 | convolution fusion | flops 6455296 | bytes 655876 | tf_op jit(solution)/shard_map/dot_general | solution.py:81
  (24 shorter events, 0.2 us)
Async XLA Ops:
  0.0 32.0 %copy-start = (bf16[64,8192]{1,0:T(8,128)(2,1)S(1)}, bf16[64,8192]{1,0:T(8,128)(2,1)}, u32[]{:S(2)}) copy-start(bf16[64,8192]{1,0:T(8,128)(2,1)} %param.25) | copy-start | bytes 3145732
  0.0 1.8 %copy-start.7 = (bf16[8,4096]{1,0:T(8,128)(2,1)S(1)}, bf16[8,4096]{1,0:T(8,128)(2,1)}, u32[]{:S(2)}) copy-start(bf16[8,4096]{1,0:T(8,128)(2,1)} %param.16) | copy-start | bytes 196612
  3.0 1.0 %copy-start.12 = (bf16[8,2,32,128]{3,2,1,0:T(8,128)(2,1)S(1)}, bf16[8,2,32,128]{3,2,1,0:T(8,128)(2,1)}, u32[]{:S(2)}) copy-start(bf16[8,2,32,128]{3,2,1,0:T(8,128)(2,1)} %param.18) | copy-start | bytes 393220
  3.3 0.7 %copy-start.11 = (bf16[8,2,128]{2,1,0:T(2,128)(2,1)S(1)}, bf16[8,2,128]{2,1,0:T(2,128)(2,1)}, u32[]{:S(2)}) copy-start(bf16[8,2,128]{2,1,0:T(2,128)(2,1)} %param.20) | copy-start | bytes 12292
  4.0 0.8 %copy-start.8 = (bf16[8,4096]{1,0:T(8,128)(2,1)S(1)}, bf16[8,4096]{1,0:T(8,128)(2,1)}, u32[]{:S(2)}) copy-start(bf16[8,4096]{1,0:T(8,128)(2,1)} %param.15) | copy-start | bytes 196612
  4.8 1.6 %copy-start.10 = (bf16[8192]{0:T(1024)(128)(2,1)S(1)}, bf16[8192]{0:T(1024)(128)(2,1)}, u32[]{:S(2)}) copy-start(bf16[8192]{0:T(1024)(128)(2,1)} %param.22) | copy-start | bytes 49156
  5.0 1.4 %collective-permute-start = (f32[8]{0:T(128)S(1)}, f32[8]{0:T(128)S(1)}, u32[]{:S(2)}, u32[]{:S(2)}) collective-permute-start(f32[8]{0:T(128)S(1)} %get-tuple-element.5), channel_id=1, source_target_pairs={{0,1},{1,0},{2,3},{3,2},{4,5},{5,4},{6,7},{7,6},{8,9},{9,8},{10,11... | collective-permute-start | bytes 104 | tf_op jit(solution)/shard_map/ppermute | solution.py:30
  5.5 0.7 %copy-start.9 = (s32[8,4]{0,1:T(4,128)S(1)}, s32[8,4]{0,1:T(4,128)}, u32[]{:S(2)}) copy-start(s32[8,4]{0,1:T(4,128)} %param.29) | copy-start | bytes 388
  6.5 1.3 %collective-permute-start.1 = (bf16[8,4096]{1,0:T(8,128)(2,1)S(1)}, bf16[8,4096]{1,0:T(8,128)(2,1)S(1)}, u32[]{:S(2)}, u32[]{:S(2)}) collective-permute-start(bf16[8,4096]{1,0:T(8,128)(2,1)S(1)} %fusion.5), channel_id=1, source_target_pairs={{0,1},{1,0},{2,3},{3,2},{4,5},{5,4},{6,7},{7,6},{8,9},{9,8},{10,11... | collective-permute-start | bytes 196616 | tf_op jit(solution)/shard_map/ppermute | solution.py:30
  7.8 0.6 %copy-start.5 = (bf16[8,4096]{1,0:T(8,128)(2,1)}, bf16[8,4096]{1,0:T(8,128)(2,1)S(1)}, u32[]{:S(2)}) copy-start(bf16[8,4096]{1,0:T(8,128)(2,1)S(1)} %collective-permute-done.1) | copy-start | bytes 196612
  9.3 16.6 %copy-start.4 = (bf16[32,8192]{1,0:T(8,128)(2,1)S(1)}, bf16[32,8192]{1,0:T(8,128)(2,1)}, u32[]{:S(2)}) copy-start(bf16[32,8192]{1,0:T(8,128)(2,1)} %param.26) | copy-start | bytes 1572868
  9.3 16.5 %all-to-all-start = ((bf16[8,2,8192]{2,1,0:T(2,128)(2,1)}), bf16[8,2,8192]{2,1,0:T(2,128)(2,1)S(1)}, u32[]{:S(2)}, u32[]{:S(2)}) async-start(bf16[8,2,8192]{2,1,0:T(2,128)(2,1)} %all_to_all.8), calls=%async_computation | async-start | bytes 524288 | tf_op jit(solution)/shard_map/all_to_all | solution.py:133
  26.0 1.0 %copy-start.3 = (bf16[32,8192]{1,0:T(8,128)(2,1)S(1)}, bf16[32,8192]{1,0:T(8,128)(2,1)}, u32[]{:S(2)}) copy-start(bf16[32,8192]{1,0:T(8,128)(2,1)} %param.28) | copy-start | bytes 1572868
  27.0 2.1 %copy-start.1 = (bf16[64,8192]{1,0:T(8,128)(2,1)S(1)}, bf16[64,8192]{1,0:T(8,128)(2,1)}, u32[]{:S(2)}) copy-start(bf16[64,8192]{1,0:T(8,128)(2,1)} %param.24) | copy-start | bytes 3145732
  28.7 1.6 %collective-permute-start.3 = (f32[16,4096]{1,0:T(8,128)S(1)}, f32[16,4096]{1,0:T(8,128)S(1)}, u32[]{:S(2)}, u32[]{:S(2)}) collective-permute-start(f32[16,4096]{1,0:T(8,128)S(1)} %constant_dynamic-slice_fusion.7), channel_id=1, source_target_pairs={{0,1},{1,0},{2,3},{3,2},{4,5},{5,4},{6,7},{7,6},{8,9},{9,8},{10,11... | collective-permute-start | bytes 786440 | tf_op jit(solution)/shard_map/ppermute | solution.py:30
  28.9 0.8 %copy-start.6 = (bf16[8,4096]{1,0:T(8,128)(2,1)S(1)}, bf16[8,4096]{1,0:T(8,128)(2,1)}, u32[]{:S(2)}) copy-start(bf16[8,4096]{1,0:T(8,128)(2,1)} %copy-done.5) | copy-start | bytes 196612
  30.2 1.9 %copy-start.2 = (bf16[64,8192]{1,0:T(8,128)(2,1)S(1)}, bf16[64,8192]{1,0:T(8,128)(2,1)}, u32[]{:S(2)}) copy-start(bf16[64,8192]{1,0:T(8,128)(2,1)} %param.23) | copy-start | bytes 3145732
  30.5 6.7 %collective-permute-start.4 = (f32[1,2,4096]{2,1,0:T(2,128)S(1)}, f32[1,2,4096]{2,1,0:T(2,128)S(1)}, u32[]{:S(2)}, u32[]{:S(2)}) collective-permute-start(f32[1,2,4096]{2,1,0:T(2,128)S(1)} %constant_dynamic-slice_fusion.6), channel_id=1, source_target_pairs={{0,2},{2,4},{4,6},{6,8},{8,10},{10,12},{12,14},{14,0},{1,3},{3,5},... | collective-permute-start | bytes 98312 | tf_op jit(solution)/shard_map/ppermute | solution.py:145
  37.3 6.1 %collective-permute-start.5 = (f32[1,2,4096]{2,1,0:T(2,128)S(1)}, f32[1,2,4096]{2,1,0:T(2,128)S(1)}, u32[]{:S(2)}, u32[]{:S(2)}) collective-permute-start(f32[1,2,4096]{2,1,0:T(2,128)S(1)} %get-tuple-element.12), channel_id=1, source_target_pairs={{0,4},{2,6},{4,8},{6,10},{8,12},{10,14},{12,0},{14,2},{1,5},{3,7},... | collective-permute-start | bytes 98312 | tf_op jit(solution)/shard_map/ppermute | solution.py:145
  37.4 11.9 %collective-permute-start.2 = (f32[8,4096]{1,0:T(8,128)S(1)}, f32[8,4096]{1,0:T(8,128)S(1)}, u32[]{:S(2)}, u32[]{:S(2)}) collective-permute-start(f32[8,4096]{1,0:T(8,128)S(1)} %constant_dynamic-slice_fusion.8), channel_id=1, source_target_pairs={{0,1},{1,0},{2,3},{3,2},{4,5},{5,4},{6,7},{7,6},{8,9},{9,8},{10,11... | collective-permute-start | bytes 393224 | tf_op jit(solution)/shard_map/ppermute | solution.py:30
  37.5 7.7 %collective-permute-start.6 = (f32[1,2,4096]{2,1,0:T(2,128)S(1)}, f32[1,2,4096]{2,1,0:T(2,128)S(1)}, u32[]{:S(2)}, u32[]{:S(2)}) collective-permute-start(f32[1,2,4096]{2,1,0:T(2,128)S(1)} %get-tuple-element.11), channel_id=1, source_target_pairs={{0,6},{2,8},{4,10},{6,12},{8,14},{10,0},{12,2},{14,4},{1,7},{3,9},... | collective-permute-start | bytes 98312 | tf_op jit(solution)/shard_map/ppermute | solution.py:145
  37.5 8.3 %collective-permute-start.7 = (f32[1,2,4096]{2,1,0:T(2,128)S(1)}, f32[1,2,4096]{2,1,0:T(2,128)S(1)}, u32[]{:S(2)}, u32[]{:S(2)}) collective-permute-start(f32[1,2,4096]{2,1,0:T(2,128)S(1)} %get-tuple-element.10), channel_id=1, source_target_pairs={{0,8},{2,10},{4,12},{6,14},{8,0},{10,2},{12,4},{14,6},{1,9},{3,11}... | collective-permute-start | bytes 98312 | tf_op jit(solution)/shard_map/ppermute | solution.py:145
  40.0 5.9 %collective-permute-start.8 = (f32[1,2,4096]{2,1,0:T(2,128)S(1)}, f32[1,2,4096]{2,1,0:T(2,128)S(1)}, u32[]{:S(2)}, u32[]{:S(2)}) collective-permute-start(f32[1,2,4096]{2,1,0:T(2,128)S(1)} %get-tuple-element.9), channel_id=1, source_target_pairs={{0,10},{2,12},{4,14},{6,0},{8,2},{10,4},{12,6},{14,8},{1,11},{3,13... | collective-permute-start | bytes 98312 | tf_op jit(solution)/shard_map/ppermute | solution.py:145
  43.4 4.4 %collective-permute-start.9 = (f32[1,2,4096]{2,1,0:T(2,128)S(1)}, f32[1,2,4096]{2,1,0:T(2,128)S(1)}, u32[]{:S(2)}, u32[]{:S(2)}) collective-permute-start(f32[1,2,4096]{2,1,0:T(2,128)S(1)} %get-tuple-element.8), channel_id=1, source_target_pairs={{0,12},{2,14},{4,0},{6,2},{8,4},{10,6},{12,8},{14,10},{1,13},{3,15... | collective-permute-start | bytes 98312 | tf_op jit(solution)/shard_map/ppermute | solution.py:145
  45.2 4.0 %collective-permute-start.10 = (f32[1,2,4096]{2,1,0:T(2,128)S(1)}, f32[1,2,4096]{2,1,0:T(2,128)S(1)}, u32[]{:S(2)}, u32[]{:S(2)}) collective-permute-start(f32[1,2,4096]{2,1,0:T(2,128)S(1)} %get-tuple-element.7), channel_id=1, source_target_pairs={{0,14},{2,0},{4,2},{6,4},{8,6},{10,8},{12,10},{14,12},{1,15},{3,1}... | collective-permute-start | bytes 98312 | tf_op jit(solution)/shard_map/ppermute | solution.py:145
